TPU v7x, 128 devices: a whole 4x4x4 slice. The times are simulated.
128 devices in a mesh: req: 32 (over x, z, core), tp: 4 (over y).
Axes of the slice: x: 4, y: 4, z: 4, core: 2. Of those that a mesh axis runs over, the one named last changes fastest.
Arguments:
- hidden: bfloat16 [8192, 2048], P('req', 'tp'), may hold values from -45 to 45
- routes: int32 [8192, 2], P('req'), may hold values from 0 to 7, all different within a row; in each aligned block of 256 rows (0 to 255, 256 to 511, ...) at most 128 rows name the same one
- route_weights: float32 [8192, 2], P('req'), may hold values from 0.2 to 1
- pre_gain: float32 [2048], replicated, may hold values from 0.1 to 1.9
- out_gain: float32 [2048], P('tp'), may hold values from 0.1 to 1.9
- gate_weight: bfloat16 [32, 2048, 5632], P('req', None, 'tp'), as said below
- up_weight: bfloat16 [32, 2048, 5632], P('req', None, 'tp'), as said below
- down_weight: bfloat16 [32, 5632, 2048], P('req', 'tp'), as said below
Outputs:
- residual_out: bfloat16 [8192, 2048], P('req', 'tp')
- normed_out: bfloat16 [8192, 2048], P('req', 'tp')
Inputs may be any that keep to these rules, and one draw needn't show every extreme that they name: `routes`: each row names 2 different experts; in the rows of one index of req no expert is named by more than 128 rows, a bound that some block reaches. `gate_weight`: index r holds expert r % 8. `up_weight`: index r holds expert r % 8. `down_weight`: index r holds expert r % 8.
All inputs are finite; a program needn't handle non-finite values.
Results may differ from a plain program's by a relative error of at most 0.007.
Values may be sent and summed in bfloat16 or wider, within the bound.
No kernel may reach another device: no remote copies, remote signals or barrier semaphores. Data moves between devices by JAX's collectives and lax.ppermute only.
A program may use at most 128 MiB of HBM per device.

v0:
```python
import jax
import jax.numpy as jnp
from jax import lax
from jax.sharding import PartitionSpec as P

E = 8
CAP = 128
epsilon = 1e-05


def shards(hidden, routes, route_weights, pre_gain, out_gain, gate_weight, up_weight, down_weight):
    row_count, col_part = hidden.shape
    tp_count = lax.axis_size("tp")
    req_count = lax.axis_size("req")
    full_width = col_part * tp_count
    copies = req_count // E
    slot_count = CAP // copies
    stream = hidden.astype(jnp.float32)
    whole_rows = lax.all_gather(hidden, "tp", axis=1, tiled=True).astype(jnp.float32)
    meansq = jnp.sum(whole_rows * whole_rows, axis=1) / full_width
    normed_in = (whole_rows * lax.rsqrt(meansq + epsilon)[:, None] * pre_gain[None, :]).astype(
        jnp.bfloat16
    )
    send_cols = normed_in.shape[1]
    chosen = routes.reshape(-1)
    onehot = (chosen[:, None] == jnp.arange(E, dtype=jnp.int32)[None, :]).astype(jnp.int32)
    slot_rank = jnp.sum((jnp.cumsum(onehot, axis=0) - 1) * onehot, axis=1)
    position = chosen * CAP + slot_rank
    entry_rows = jnp.arange(chosen.shape[0], dtype=jnp.int32) // routes.shape[1]
    slot_row = jnp.zeros((E * CAP,), jnp.int32).at[position].set(entry_rows)
    slot_live = jnp.zeros((E * CAP,), jnp.bool_).at[position].set(True)
    outgoing = jnp.where(slot_live[:, None], normed_in[slot_row], jnp.zeros((), jnp.bfloat16))
    outgoing = outgoing.reshape(E, slot_count, copies, send_cols).transpose(2, 0, 1, 3)
    outgoing = outgoing.reshape(req_count, slot_count, send_cols)
    pieces = lax.all_to_all(outgoing, "req", split_axis=0, concat_axis=0, tiled=True)
    sources, items, widths = pieces.shape
    flat_rows = pieces.reshape(sources * items, widths)
    gate_val = jnp.dot(flat_rows, gate_weight[0], preferred_element_type=jnp.float32)
    up_val = jnp.dot(flat_rows, up_weight[0], preferred_element_type=jnp.float32)
    activ = (jax.nn.silu(gate_val) * up_val).astype(jnp.bfloat16)
    partial_out = jnp.dot(activ, down_weight[0], preferred_element_type=jnp.float32)
    partial_out = lax.optimization_barrier(partial_out.astype(jnp.bfloat16)).astype(jnp.float32)
    summed = lax.psum_scatter(
        partial_out.reshape(sources, items, widths).astype(jnp.bfloat16),
        "tp",
        scatter_dimension=2,
        tiled=True,
    )
    returned = lax.all_to_all(summed, "req", split_axis=0, concat_axis=0, tiled=True)
    returned = returned.reshape(copies, E, slot_count, col_part).transpose(1, 2, 0, 3)
    returned = returned.reshape(E * CAP, col_part)
    picked = returned[position].reshape(row_count, routes.shape[1], col_part).astype(jnp.float32)
    mixed = jnp.sum(picked * route_weights[:, :, None], axis=1)
    total_stream = stream + mixed
    out_sums = lax.psum(jnp.sum(total_stream * total_stream, axis=1), "tp")
    normed_out = (
        total_stream * lax.rsqrt(out_sums / full_width + epsilon)[:, None] * out_gain[None, :]
    )
    return (total_stream.astype(jnp.bfloat16), normed_out.astype(jnp.bfloat16))


def solution(mesh):
    return jax.shard_map(
        shards,
        mesh=mesh,
        in_specs=(
            P("req", "tp"),
            P("req", None),
            P("req", None),
            P(),
            P("tp"),
            P("req", None, "tp"),
            P("req", None, "tp"),
            P("req", "tp", None),
        ),
        out_specs=(P("req", "tp"), P("req", "tp")),
        check_vma=False,
    )
```

profile of v0, /device:TPU:0, one launch (start us, length us, event | category | flops | bytes accessed | tf_op | source)
XLA Modules:
  0.0 241.1 jit_solution(10688515270769743538)
XLA Ops:
  7.2 0.7 all-gather.2.cloned.1.call-update
  7.9 0.8 copy.13
  9.1 1.1 reduce-window.6
  10.5 0.7 broadcast_multiply_fusion
  11.6 2.4 %scatter_custom_fusion.1 = s32[1024]{0:T(1024)S(1)} fusion(s32[512]{0:T(512)S(1)} %bitcast.42, s32[512]{0:T(512)S(1)} %add_select_fusion, s32[]{:T(128)} %constant.37.clone.1), kind=kCustom, calls=%fused_computation.41 | custom fusion | bytes 4100 | tf_op jit(solution)/shard_map/scatter | solution.py:30
  14.0 2.4 %scatter_custom_fusion = pred[1024]{0:T(1024)(128)(4,1)S(1)} fusion(s32[512]{0:T(512)S(1)} %bitcast.43, pred[512]{0:T(512)(128)(4,1)S(1)} %broadcast.99, pred[]{:T(512)} %constant.20.clone.1), kind=kCustom, calls=%fused_computation.44 | custom fusion | bytes 1025 | tf_op jit(solution)/shard_map/scatter | solution.py:31
  16.8 19.4 %all-gather.2.cloned.1.call-done = bf16[256,2048]{1,0:T(8,128)(2,1)} async-done(((bf16[256,512]{1,0:T(8,128)(2,1)}), bf16[256,2048]{1,0:T(8,128)(2,1)}) %all-gather.2.cloned.1.call-update) | async-done | bytes 1048592 | tf_op jit(solution)/shard_map/all_gather | solution.py:19
  36.1 1.5 fusion.16
  37.7 1.5 fusion.18
  39.2 6.0 %gather_fusion = bf16[1024,2048]{1,0:T(8,128)(2,1)} fusion(bf16[256,2048]{1,0:T(8,128)(2,1)S(1)} %fusion.18, s32[1024]{0:T(1024)S(1)} %fusion.22), kind=kCustom, calls=%fused_computation | custom fusion | bytes 8392704 | tf_op jit(solution)/shard_map/gather | solution.py:32
  45.2 7.2 %gather.9 = bf16[8,32,4,2048]{3,2,1,0:T(4,128)(2,1)} reshape(bf16[1024,2048]{1,0:T(8,128)(2,1)} %gather_fusion) | data formatting | bytes 8388608 | tf_op jit(solution)/shard_map/gather | solution.py:32
  52.4 8.5 %copy_select_fusion = bf16[8,32,4,2048]{3,1,0,2:T(8,128)(2,1)S(1)} fusion(bf16[8,32,4,2048]{3,2,1,0:T(4,128)(2,1)} %gather.9, pred[8,32,4]{1,0,2:T(8,128)(4,1)S(1)} %copy.15), kind=kLoop, calls=%fused_computation.11 | loop fusion | flops 2097152 | bytes 8389632 | tf_op jit(solution)/shard_map/jit(_where)/select_n | solution.py:32
  60.9 57.5 %all_to_all.10 = bf16[32,32,2048]{2,1,0:T(8,128)(2,1)S(1)} all-to-all(bf16[32,32,2048]{2,1,0:T(8,128)(2,1)S(1)} %bitcast.36), channel_id=1, replica_groups=mesh['req'=32,'tp'=4] {'req'}, dimensions={0} | all-to-all | bytes 8388608 | tf_op jit(solution)/shard_map/all_to_all | solution.py:35
  118.4 2.1 copy-done
  120.5 10.2 %fusion.4 = f32[1024,1408]{1,0:T(8,128)} fusion(bf16[1024,2048]{1,0:T(8,128)(2,1)S(1)} %bitcast.38, bf16[1,2048,1408]{2,1,0:T(8,128)(2,1)} %param.13), kind=kOutput, calls=%fused_computation.8 | convolution fusion | flops 5905580032 | bytes 15728640 | tf_op jit(solution)/shard_map/dot_general | solution.py:38
  130.8 20.6 %fusion.10 = bf16[1024,2048]{1,0:T(8,128)(2,1)} fusion(bf16[1,1408,2048]{2,1,0:T(8,128)(2,1)} %param.15, f32[1024,1408]{1,0:T(8,128)} %fusion.4, bf16[1024,2048]{1,0:T(8,128)(2,1)} %bitcast.39, bf16[1,2048,1408]{2,1,0:T(8,128)(2,1)} %param.14), kind=kOutput, calls=%fused_computation.12 | convolution fusion | flops 11821907968 | bytes 25690112 | tf_op jit(solution)/shard_map/dot_general | solution.py:41
  151.4 44.1 %reduce-scatter.2.cloned.1.call-done = bf16[32,32,512]{2,1,0:T(8,128)(2,1)} async-done(((bf16[32,32,2048]{2,1,0:T(8,128)(2,1)}), bf16[32,32,512]{2,1,0:T(8,128)(2,1)}) %reduce-scatter.2.cloned.1.call-update) | async-done | bytes 1048592 | tf_op jit(solution)/shard_map/reduce_scatter | solution.py:43
  195.5 7.2 %all-to-all-start.1 = ((bf16[32,32,512]{2,1,0:T(8,128)(2,1)}), bf16[32,32,512]{2,1,0:T(8,128)(2,1)S(1)}, u32[]{:S(2)}, u32[]{:S(2)}) async-start(bf16[32,32,512]{2,1,0:T(8,128)(2,1)} %reduce-scatter.2.cloned.1.call-done), calls=%async_computation.2 | async-start | bytes 2097152 | tf_op jit(solution)/shard_map/all_to_all | solution.py:49
  202.9 16.6 %all-to-all-done.1 = bf16[32,32,512]{2,1,0:T(8,128)(2,1)S(1)} async-done(((bf16[32,32,512]{2,1,0:T(8,128)(2,1)}), bf16[32,32,512]{2,1,0:T(8,128)(2,1)S(1)}, u32[]{:S(2)}, u32[]{:S(2)}) %all-to-all-start.1) | async-done | bytes 1048608 | tf_op jit(solution)/shard_map/all_to_all | solution.py:49
  219.6 0.8 copy.21
  220.7 2.0 gather_fusion.1
  223.4 1.3 multiply_reduce_fusion
  224.8 8.6 %psum.7 = f32[256]{0:T(256)S(1)} all-reduce(f32[256]{0:T(256)S(1)} %multiply_reduce_fusion.1), channel_id=1, replica_groups=mesh['req'=32,'tp'=4] {'tp'}, use_global_device_ids=true, to_apply=%region_9.10 | all-reduce | flops 256 | bytes 2048 | tf_op jit(solution)/shard_map/psum | solution.py:55
  233.4 0.8 multiply_convert_fusion.1
  (32 shorter events, 2.6 us)
Async XLA Ops:
  7.2 29.0 %all-gather.2.cloned.1.call-start = ((), (), s32[]{:S(2)}) async-start(), calls=%async_computation.3 | async-start | bytes 1310720 | tf_op jit(solution)/shard_map/all_gather | solution.py:19
  7.9 187.6 %reduce-scatter.2.cloned.1.call-start = ((), (), s32[]{:S(2)}) async-start(), calls=%async_computation.4 | async-start | bytes 5242880 | tf_op jit(solution)/shard_map/reduce_scatter | solution.py:43
  118.4 2.1 copy-start
  151.4 51.4 %copy-start.2 = (f32[256,2]{0,1:T(2,128)S(1)}, f32[256,2]{0,1:T(2,128)}, u32[]{:S(2)}) copy-start(f32[256,2]{0,1:T(2,128)} %param.10) | copy-start | bytes 6148
  195.5 24.1 %all-to-all-start.1 = ((bf16[32,32,512]{2,1,0:T(8,128)(2,1)}), bf16[32,32,512]{2,1,0:T(8,128)(2,1)S(1)}, u32[]{:S(2)}, u32[]{:S(2)}) async-start(bf16[32,32,512]{2,1,0:T(8,128)(2,1)} %reduce-scatter.2.cloned.1.call-done), calls=%async_computation.2 | async-start | bytes 2097152 | tf_op jit(solution)/shard_map/all_to_all | solution.py:49
  220.7 4.0 %copy-start.1 = (bf16[256,512]{1,0:T(8,128)(2,1)S(1)}, bf16[256,512]{1,0:T(8,128)(2,1)}, u32[]{:S(2)}) copy-start(bf16[256,512]{1,0:T(8,128)(2,1)} %param.8) | copy-start | bytes 786436
  220.7 12.7 %copy-start.3 = (f32[512]{0:T(512)S(1)}, f32[512]{0:T(512)}, u32[]{:S(2)}) copy-start(f32[512]{0:T(512)} %param.12) | copy-start | bytes 6148
Sparse Core Ops, SparseCore 0:
  9.7 26.4 all-gather.1
  151.5 43.9 reduce-scatter.1
where the time goes:
time: 242 us; the launch traced here: 241 us
  waiting for transfers between devices  80.8 us (33%)
  blocking collectives  66.1 us (27%)
  matrix products  30.9 us (13%)
  local copies, waits for them, and re-layouts  26 us (11%)
  other arithmetic  15.8 us (7%)
  between operations  14.2 us (6%)
  starting transfers between devices  7.31 us (3%)
    all_to_all x1, blocking collectives, shards(): lax.all_to_all(outgoing, 'req', split_axis=0, concat_axis=0, tiled=True)  57.5 us
    reduce_scatter x1, waiting for transfers between devices, shards(): lax.psum_scatter(partial_out.reshape(sources, items, widths).astype(jnp.b...  44.1 us
    dot_general x1, matrix products, shards(): jnp.dot(activ, down_weight[0], preferred_element_type=jnp.float32)  20.6 us
    all_gather x1, waiting for transfers between devices, shards(): lax.all_gather(hidden, 'tp', axis=1, tiled=True).astype(jnp.float32)  19.4 us
    all_to_all x1, waiting for transfers between devices, shards(): lax.all_to_all(summed, 'req', split_axis=0, concat_axis=0, tiled=True)  16.6 us
    gather x2, local copies, waits for them, and re-layouts, shards(): normed_in[slot_row]  13.2 us
    dot_general x1, matrix products, shards(): jnp.dot(flat_rows, gate_weight[0], preferred_element_type=jnp.float32)  10.2 us
    psum x1, blocking collectives, shards(): out_sums = lax.psum(jnp.sum(total_stream * total_stream, axis=1), 'tp')  8.58 us
  transfers between devices with their start and end apart: 3, of which 3 were waited for; matrix products, arithmetic and copies ran while one was open for 4% of the time, Pallas kernels for 0%

commit v1 on v0

--- a/solution.py
+++ b/solution.py
@@ -8,6 +8,19 @@
 epsilon = 1e-05
 
 
+def collect(value, axis, dim):
+    ways = lax.axis_size(axis)
+    up = [(d, (d + 1) % ways) for d in range(ways)]
+    down = [(d, (d - 1) % ways) for d in range(ways)]
+    earlier, later = ([value], [value])
+    for _ in range(ways // 2):
+        earlier.append(lax.ppermute(earlier[-1], axis, up))
+    for _ in range((ways - 1) // 2):
+        later.append(lax.ppermute(later[-1], axis, down))
+    line = jnp.concatenate([*earlier[::-1], *later[1:]], axis=dim)
+    return jnp.roll(line, (lax.axis_index(axis) - ways // 2) * value.shape[dim], axis=dim)
+
+
 def shards(hidden, routes, route_weights, pre_gain, out_gain, gate_weight, up_weight, down_weight):
     row_count, col_part = hidden.shape
     tp_count = lax.axis_size("tp")
@@ -16,7 +29,7 @@
     copies = req_count // E
     slot_count = CAP // copies
     stream = hidden.astype(jnp.float32)
-    whole_rows = lax.all_gather(hidden, "tp", axis=1, tiled=True).astype(jnp.float32)
+    whole_rows = collect(hidden, "tp", 1).astype(jnp.float32)
     meansq = jnp.sum(whole_rows * whole_rows, axis=1) / full_width
     normed_in = (whole_rows * lax.rsqrt(meansq + epsilon)[:, None] * pre_gain[None, :]).astype(
         jnp.bfloat16

time: 242 us -> 229 us (0.946)
  waiting for transfers between devices: 80.8 us -> 65.2 us
  starting transfers between devices: 7.31 us -> 10.9 us
    all_gather x1 -> x0, waiting for transfers between devices: 19.4 us -> none  [shards(): lax.all_gather(hidden, 'tp', axis=1, tiled=True).astype(jnp.float32)]
    ppermute x0 -> x3, waiting for transfers between devices: none -> 5.83 us  [the longest x2 5.83 us: collect(): earlier.append(lax.ppermute(earlier[-1], axis, up))]
    ppermute x0 -> x3, starting transfers between devices: none -> 3.61 us  [the longest x2 2.03 us: collect(): earlier.append(lax.ppermute(earlier[-1], axis, up))]
  transfers between devices with their start and end apart: 3 -> 5, of which waited for: 3 -> 4; matrix products, arithmetic and copies ran while one was open for 4% -> 4% of each run, Pallas kernels for 0% -> 0%
where the time goes in v1:
time: 229 us
  blocking collectives  66.9 us (29%)
  waiting for transfers between devices  65.2 us (28%)
  matrix products  30.9 us (13%)
  local copies, waits for them, and re-layouts  27.1 us (12%)
  between operations  14.3 us (6%)
  other arithmetic  13.4 us (6%)
  starting transfers between devices  10.9 us (5%)
    all_to_all x1, blocking collectives, shards(): lax.all_to_all(outgoing, 'req', split_axis=0, concat_axis=0, tiled=True)  58.4 us
    reduce_scatter x1, waiting for transfers between devices, shards(): lax.psum_scatter(partial_out.reshape(sources, items, widths).astype(jnp.b...  42.7 us
    dot_general x1, matrix products, shards(): jnp.dot(activ, down_weight[0], preferred_element_type=jnp.float32)  20.6 us
    all_to_all x1, waiting for transfers between devices, shards(): lax.all_to_all(summed, 'req', split_axis=0, concat_axis=0, tiled=True)  16.6 us
    gather x2, local copies, waits for them, and re-layouts, shards(): normed_in[slot_row]  13.2 us
    dot_general x1, matrix products, shards(): jnp.dot(flat_rows, gate_weight[0], preferred_element_type=jnp.float32)  10.2 us
    psum x1, blocking collectives, shards(): out_sums = lax.psum(jnp.sum(total_stream * total_stream, axis=1), 'tp')  8.56 us
    select_n x1, other arithmetic, shards(): jnp.where(slot_live[:, None], normed_in[slot_row], jnp.zeros((), jnp.bflo...  8.47 us
  transfers between devices with their start and end apart: 5, of which 4 were waited for; matrix products, arithmetic and copies ran while one was open for 4% of the time, Pallas kernels for 0%

profile of v1, /device:TPU:0, one launch (start us, length us, event | category | flops | bytes accessed | tf_op | source)
XLA Modules:
  0.0 228.6 jit_solution(11939216720685359319)
XLA Ops:
  7.2 1.7 collective-permute-start
  9.0 1.6 collective-permute-start.2
  10.5 0.8 copy.13
  12.3 1.1 reduce-window.6
  14.1 2.8 %collective-permute-done = bf16[256,512]{1,0:T(8,128)(2,1)S(1)} collective-permute-done((bf16[256,512]{1,0:T(8,128)(2,1)}, bf16[256,512]{1,0:T(8,128)(2,1)S(1)}, u32[]{:S(2)}, u32[]{:S(2)}) %collective-permute-start) | collective-permute-done | bytes 262176 | tf_op jit(solution)/shard_map/ppermute | solution.py:17
  17.2 2.4 %scatter_custom_fusion.1 = s32[1024]{0:T(1024)S(1)} fusion(s32[512]{0:T(512)S(1)} %bitcast.42, s32[512]{0:T(512)S(1)} %add_select_fusion, s32[]{:T(128)} %constant.60.clone.1), kind=kCustom, calls=%fused_computation.49 | custom fusion | bytes 4100 | tf_op jit(solution)/shard_map/scatter | solution.py:43
  19.7 2.4 %scatter_custom_fusion = pred[1024]{0:T(1024)(128)(4,1)S(1)} fusion(s32[512]{0:T(512)S(1)} %bitcast.43, pred[512]{0:T(512)(128)(4,1)S(1)} %broadcast.100, pred[]{:T(512)} %constant.58.clone.1), kind=kCustom, calls=%fused_computation.52 | custom fusion | bytes 1025 | tf_op jit(solution)/shard_map/scatter | solution.py:44
  22.4 3.0 %collective-permute-done.1 = bf16[256,512]{1,0:T(8,128)(2,1)S(1)} collective-permute-done((bf16[256,512]{1,0:T(8,128)(2,1)S(1)}, bf16[256,512]{1,0:T(8,128)(2,1)S(1)}, u32[]{:S(2)}, u32[]{:S(2)}) %collective-permute-start.1) | collective-permute-done | bytes 262176 | tf_op jit(solution)/shard_map/ppermute | solution.py:17
  25.5 1.0 constant_dynamic-update-slice_fusion.5
  27.3 6.0 %gather_fusion = bf16[1024,2048]{1,0:T(8,128)(2,1)} fusion(bf16[256,2048]{1,0:T(8,128)(2,1)S(1)} %fusion.18, s32[1024]{0:T(1024)S(1)} %fusion.22), kind=kCustom, calls=%fused_computation | custom fusion | bytes 8392704 | tf_op jit(solution)/shard_map/gather | solution.py:45
  33.3 7.2 %gather.9 = bf16[8,32,4,2048]{3,2,1,0:T(4,128)(2,1)} reshape(bf16[1024,2048]{1,0:T(8,128)(2,1)} %gather_fusion) | data formatting | bytes 8388608 | tf_op jit(solution)/shard_map/gather | solution.py:45
  40.5 8.5 %copy_select_fusion = bf16[8,32,4,2048]{3,1,0,2:T(8,128)(2,1)S(1)} fusion(bf16[8,32,4,2048]{3,2,1,0:T(4,128)(2,1)} %gather.9, pred[8,32,4]{1,0,2:T(8,128)(4,1)S(1)} %copy.15), kind=kLoop, calls=%fused_computation.11 | loop fusion | flops 2097152 | bytes 8389632 | tf_op jit(solution)/shard_map/jit(_where)/select_n | solution.py:45
  49.0 58.4 %all_to_all.10 = bf16[32,32,2048]{2,1,0:T(8,128)(2,1)S(1)} all-to-all(bf16[32,32,2048]{2,1,0:T(8,128)(2,1)S(1)} %bitcast.36), channel_id=1, replica_groups=mesh['req'=32,'tp'=4] {'req'}, dimensions={0} | all-to-all | bytes 8388608 | tf_op jit(solution)/shard_map/all_to_all | solution.py:48
  107.4 2.1 copy-done
  109.5 10.2 %fusion.4 = f32[1024,1408]{1,0:T(8,128)} fusion(bf16[1024,2048]{1,0:T(8,128)(2,1)S(1)} %bitcast.38, bf16[1,2048,1408]{2,1,0:T(8,128)(2,1)} %param.13), kind=kOutput, calls=%fused_computation.8 | convolution fusion | flops 5905580032 | bytes 15728640 | tf_op jit(solution)/shard_map/dot_general | solution.py:51
  119.7 20.6 %fusion.10 = bf16[1024,2048]{1,0:T(8,128)(2,1)} fusion(bf16[1,1408,2048]{2,1,0:T(8,128)(2,1)} %param.15, f32[1024,1408]{1,0:T(8,128)} %fusion.4, bf16[1024,2048]{1,0:T(8,128)(2,1)} %bitcast.39, bf16[1,2048,1408]{2,1,0:T(8,128)(2,1)} %param.14), kind=kOutput, calls=%fused_computation.12 | convolution fusion | flops 11821907968 | bytes 25690112 | tf_op jit(solution)/shard_map/dot_general | solution.py:54
  140.4 42.7 %reduce-scatter.2.cloned.1.call-done = bf16[32,32,512]{2,1,0:T(8,128)(2,1)} async-done(((bf16[32,32,2048]{2,1,0:T(8,128)(2,1)}), bf16[32,32,512]{2,1,0:T(8,128)(2,1)}) %reduce-scatter.2.cloned.1.call-update) | async-done | bytes 1048592 | tf_op jit(solution)/shard_map/reduce_scatter | solution.py:56
  183.1 7.2 %all-to-all-start.1 = ((bf16[32,32,512]{2,1,0:T(8,128)(2,1)}), bf16[32,32,512]{2,1,0:T(8,128)(2,1)S(1)}, u32[]{:S(2)}, u32[]{:S(2)}) async-start(bf16[32,32,512]{2,1,0:T(8,128)(2,1)} %reduce-scatter.2.cloned.1.call-done), calls=%async_computation.2 | async-start | bytes 2097152 | tf_op jit(solution)/shard_map/all_to_all | solution.py:62
  190.5 16.6 %all-to-all-done.1 = bf16[32,32,512]{2,1,0:T(8,128)(2,1)S(1)} async-done(((bf16[32,32,512]{2,1,0:T(8,128)(2,1)}), bf16[32,32,512]{2,1,0:T(8,128)(2,1)S(1)}, u32[]{:S(2)}, u32[]{:S(2)}) %all-to-all-start.1) | async-done | bytes 1048608 | tf_op jit(solution)/shard_map/all_to_all | solution.py:62
  207.1 0.8 copy.21
  208.3 2.0 gather_fusion.1
  210.9 1.3 multiply_reduce_fusion
  212.4 8.6 %psum.7 = f32[256]{0:T(256)S(1)} all-reduce(f32[256]{0:T(256)S(1)} %multiply_reduce_fusion.1), channel_id=1, replica_groups=mesh['req'=32,'tp'=4] {'tp'}, use_global_device_ids=true, to_apply=%region_9.10 | all-reduce | flops 256 | bytes 2048 | tf_op jit(solution)/shard_map/psum | solution.py:68
  220.9 0.8 multiply_convert_fusion.1
  (45 shorter events, 4.3 us)
Async XLA Ops:
  7.2 19.5 %copy-start.1 = (bf16[256,512]{1,0:T(8,128)(2,1)S(1)}, bf16[256,512]{1,0:T(8,128)(2,1)}, u32[]{:S(2)}) copy-start(bf16[256,512]{1,0:T(8,128)(2,1)} %param.8) | copy-start | bytes 786436
  7.2 19.8 %copy-start.2 = (f32[2048]{0:T(1024)S(1)}, f32[2048]{0:T(1024)}, u32[]{:S(2)}) copy-start(f32[2048]{0:T(1024)} %param.11) | copy-start | bytes 24580
  7.2 175.9 %reduce-scatter.2.cloned.1.call-start = ((), (), s32[]{:S(2)}) async-start(), calls=%async_computation.3 | async-start | bytes 5242880 | tf_op jit(solution)/shard_map/reduce_scatter | solution.py:56
  7.2 9.7 %collective-permute-start = (bf16[256,512]{1,0:T(8,128)(2,1)}, bf16[256,512]{1,0:T(8,128)(2,1)S(1)}, u32[]{:S(2)}, u32[]{:S(2)}) collective-permute-start(bf16[256,512]{1,0:T(8,128)(2,1)} %param.8), channel_id=1, source_target_pairs={{0,1},{1,2},{2,3},{3,0},{4,5},{5,6},{6,7},{7,4},{8,9},{9,10},{10,1... | collective-permute-start | bytes 786440 | tf_op jit(solution)/shard_map/ppermute | solution.py:17
  9.0 17.6 %collective-permute-start.2 = (bf16[256,512]{1,0:T(8,128)(2,1)}, bf16[256,512]{1,0:T(8,128)(2,1)S(1)}, u32[]{:S(2)}, u32[]{:S(2)}) collective-permute-start(bf16[256,512]{1,0:T(8,128)(2,1)} %param.8), channel_id=1, source_target_pairs={{0,3},{1,0},{2,1},{3,2},{4,7},{5,4},{6,5},{7,6},{8,11},{9,8},{10,9... | collective-permute-start | bytes 786440 | tf_op jit(solution)/shard_map/ppermute | solution.py:19
  16.9 8.6 %collective-permute-start.1 = (bf16[256,512]{1,0:T(8,128)(2,1)S(1)}, bf16[256,512]{1,0:T(8,128)(2,1)S(1)}, u32[]{:S(2)}, u32[]{:S(2)}) collective-permute-start(bf16[256,512]{1,0:T(8,128)(2,1)S(1)} %collective-permute-done), channel_id=1, source_target_pairs={{0,1},{1,2},{2,3},{3,0},{4,5},{5,6},{6,7},{7,4},{8,9},{9,10},{10,1... | collective-permute-start | bytes 786440 | tf_op jit(solution)/shard_map/ppermute | solution.py:17
  107.4 2.1 copy-start
  140.3 50.0 %copy-start.3 = (f32[256,2]{0,1:T(2,128)S(1)}, f32[256,2]{0,1:T(2,128)}, u32[]{:S(2)}) copy-start(f32[256,2]{0,1:T(2,128)} %param.10) | copy-start | bytes 6148
  183.1 24.1 %all-to-all-start.1 = ((bf16[32,32,512]{2,1,0:T(8,128)(2,1)}), bf16[32,32,512]{2,1,0:T(8,128)(2,1)S(1)}, u32[]{:S(2)}, u32[]{:S(2)}) async-start(bf16[32,32,512]{2,1,0:T(8,128)(2,1)} %reduce-scatter.2.cloned.1.call-done), calls=%async_computation.2 | async-start | bytes 2097152 | tf_op jit(solution)/shard_map/all_to_all | solution.py:62
  208.2 12.7 %copy-start.4 = (f32[512]{0:T(512)S(1)}, f32[512]{0:T(512)}, u32[]{:S(2)}) copy-start(f32[512]{0:T(512)} %param.12) | copy-start | bytes 6148
Sparse Core Ops, SparseCore 0:
  140.5 42.5 reduce-scatter.1
